TPU v7x, 512 devices: a whole 4x4x16 slice. The times are simulated.
512 devices in a mesh: ctx: 64 (over z, y), tp: 8 (over x, core).
Axes of the slice: x: 4, y: 4, z: 16, core: 2. Of those that a mesh axis runs over, the one named last changes fastest.
Arguments:
- features: bfloat16 [3, 4096, 8192], P(None, 'ctx', 'tp'), may hold values from -6 to 6
- short_weight: float32 [3, 3, 8192], P(None, None, 'tp'), may hold values from -3 to 3
- decay_rate: float32 [512, 16], P('tp'), may hold values from 0.00012207031 to 0.03
- residue: float32 [512, 16], P('tp'), may hold values from -3 to 3
- skip_gain: float32 [8192], P('tp'), may hold values from -1 to 1
- out_weight: bfloat16 [8192, 4096], P('tp', 'ctx'), may hold values from -0.1875 to 0.1875
Outputs:
- mixed_out: bfloat16 [4096, 4096], P('ctx', 'tp')
All inputs are finite; a program needn't handle non-finite values.
Results may differ from a plain program's by a relative error of at most 0.006.
Values may be sent and summed in bfloat16 or wider, within the bound.
No kernel may reach another device: no remote copies, remote signals or barrier semaphores. Data moves between devices by JAX's collectives and lax.ppermute only.
A program may use at most 128 MiB of HBM per device.

v0:
```python
import jax
import jax.numpy as jnp
import numpy as np
from jax import lax
from jax.sharding import Mesh
from jax.sharding import PartitionSpec as P

CTX = ("chi", "clo")


def shifted(value, axis, count, by):
    pairs = [(i, i + by) for i in range(count) if i + by < count]
    return lax.ppermute(value, axis, pairs)


def rotated(value, axis, count, by):
    return lax.ppermute(value, axis, [(i, (i + by) % count) for i in range(count)])


def digit_rotated(value, count, stride, size, by):
    pairs = []
    for i in range(count):
        d = i // stride % size
        pairs.append((i, i + ((d + by) % size - d) * stride))
    return lax.ppermute(value, CTX, pairs)


def scan_levels(count):
    levels = []
    while count > 1:
        size = 4 if count % 4 == 0 else count
        levels.append(size)
        count //= size
    return levels


def make_per_device(n_ctx, n_tp):
    n_lo = n_ctx // n_tp

    def per_device(features, short_weight, decay_rate, residue, skip_gain, out_weight):
        rows = features.shape[1]
        chans = features.shape[2]
        groups = decay_rate.shape[0]
        width = chans // groups
        taps = short_weight.shape[1]
        chi = lax.axis_index("chi")
        clo = lax.axis_index("clo")
        me = chi * n_lo + clo
        tp = lax.axis_index("tp")
        weight = lax.all_gather(out_weight, "chi", axis=1, tiled=True)
        weight = weight.reshape(chans, n_tp, -1)
        rim = shifted(features[:, rows - (taps - 1) :, :], CTX, n_ctx, 1)
        extended = jnp.concatenate([rim, features], axis=1)
        conv = jnp.zeros(features.shape, jnp.float32)
        for j in range(taps):
            conv = conv + short_weight[:, j][:, None, :] * extended[
                :, taps - 1 - j : taps - 1 - j + rows, :
            ].astype(jnp.float32)
        q_lane = conv[0]
        gated = (conv[1] * conv[2]).astype(jnp.bfloat16)
        gated_wide = gated.astype(jnp.float32)
        coef = residue * jnp.sqrt(-jnp.expm1(-2.0 * decay_rate))
        lags = jnp.arange(rows, dtype=jnp.float32)
        near_filter = jnp.sum(
            coef[:, :, None] * jnp.exp(-decay_rate[:, :, None] * lags[None, None, :]), axis=1
        ).astype(jnp.bfloat16)
        index = np.arange(rows)
        onehot = (index[None, :, None] - index[None, None, :] == index[:, None, None]).astype(
            np.float32
        )
        onehot = jnp.asarray(onehot.reshape(rows, rows * rows), jnp.bfloat16)
        toeplitz = jnp.dot(near_filter, onehot, preferred_element_type=jnp.float32)
        toeplitz = toeplitz.astype(jnp.bfloat16).reshape(groups, rows, rows)
        near = jnp.einsum(
            "gts,sgw->tgw",
            toeplitz,
            gated.reshape(rows, groups, width),
            preferred_element_type=jnp.float32,
        ).reshape(rows, chans)
        rate_c = jnp.repeat(decay_rate.T, width, axis=1)
        coef_c = jnp.repeat(coef.T, width, axis=1)

        def decay(blocks):
            return jnp.exp(-rate_c * (rows * blocks.astype(jnp.float32)))

        end_basis = jnp.exp(-rate_c[None] * (rows - 1.0 - lags)[:, None, None])
        own_state = jnp.sum(end_basis * gated_wide[:, None, :], axis=0)
        before = jnp.zeros_like(own_state)
        total = own_state
        stride = 1
        for size in scan_levels(n_ctx):
            d = me // stride % size
            r = me % stride
            merged = decay((size - 1 - d) * stride) * total
            for by in range(1, size):
                got = digit_rotated(total, n_ctx, stride, size, by)
                src = (d - by) % size
                before = before + jnp.where(
                    by <= d, decay((by - 1) * stride + r) * got, jnp.zeros_like(got)
                )
                merged = merged + decay((size - 1 - src) * stride) * got
            total = merged
            stride *= size
        far_basis = coef_c[None] * jnp.exp(-rate_c[None] * (lags + 1.0)[:, None, None])
        far = jnp.sum(far_basis * before[None], axis=1)
        mixed = (q_lane * (near + far + skip_gain[None, :] * gated_wide)).astype(jnp.bfloat16)
        spread = jnp.broadcast_to(mixed[None], (n_lo,) + mixed.shape)
        tokens = lax.all_to_all(spread, "clo", 0, 0, tiled=True)
        partial = jnp.einsum("ktc,cqo->qkto", tokens, weight, preferred_element_type=jnp.float32)
        pieces = lax.all_to_all(partial, "tp", 0, 0, tiled=True)
        summed = jnp.sum(pieces, axis=0).astype(jnp.bfloat16)
        back = lax.all_to_all(summed, "clo", 0, 0, tiled=True)
        return back.transpose(1, 0, 2).reshape(rows, -1)

    return per_device


def solution(mesh):
    n_ctx = mesh.shape["ctx"]
    n_tp = mesh.shape["tp"]
    devices = np.asarray(mesh.devices).reshape(n_tp, n_ctx // n_tp, n_tp)
    split = Mesh(devices, ("chi", "clo", "tp"))
    placed = (
        P(None, CTX, "tp"),
        P(None, None, "tp"),
        P("tp", None),
        P("tp", None),
        P("tp"),
        P("tp", CTX),
    )
    return jax.shard_map(
        make_per_device(n_ctx, n_tp),
        mesh=split,
        in_specs=placed,
        out_specs=P(CTX, "tp"),
        check_vma=False,
    )
```

profile of v0, /device:TPU:2, one launch (start us, length us, event | category | flops | bytes accessed | tf_op | source)
XLA Modules:
  0.0 183.9 jit_solution(3685164026990246933)
XLA Ops:
  6.5 0.8 slice.29
  7.4 3.5 %collective-permute-start = (bf16[3,2,1024]{2,1,0:T(2,128)(2,1)S(1)}, bf16[3,2,1024]{2,1,0:T(2,128)(2,1)S(1)}, u32[]{:S(2)}, u32[]{:S(2)}) collective-permute-start(bf16[3,2,1024]{2,1,0:T(2,128)(2,1)S(1)} %slice.29), channel_id=1, source_target_pairs={{0,8},{8,16},{16,24},{24,32},{32,40},{40,48},{48,56},{56,64},{64,7... | collective-permute-start | bytes 36872 | tf_op jit(solution)/shard_map/ppermute | solution.py:13
  10.8 0.9 fusion.9
  11.8 0.7 negate_bitcast_fusion
  13.6 1.8 multiply_add_fusion
  15.5 0.7 multiply_reduce_fusion.1
  16.2 3.5 %collective-permute-start.1 = (f32[16,1024]{1,0:T(8,128)S(1)}, f32[16,1024]{1,0:T(8,128)S(1)}, u32[]{:S(2)}, u32[]{:S(2)}) collective-permute-start(f32[16,1024]{1,0:T(8,128)S(1)} %multiply_reduce_fusion.1), channel_id=1, source_target_pairs={{0,8},{8,16},{16,24},{24,0},{32,40},{40,48},{48,56},{56,32},{64,72... | collective-permute-start | bytes 196616 | tf_op jit(solution)/shard_map/ppermute | solution.py:25
  19.7 4.8 %collective-permute-start.2 = (f32[16,1024]{1,0:T(8,128)S(1)}, f32[16,1024]{1,0:T(8,128)S(1)}, u32[]{:S(2)}, u32[]{:S(2)}) collective-permute-start(f32[16,1024]{1,0:T(8,128)S(1)} %multiply_reduce_fusion.1), channel_id=1, source_target_pairs={{0,16},{8,24},{16,0},{24,8},{32,48},{40,56},{48,32},{56,40},{64,80... | collective-permute-start | bytes 196616 | tf_op jit(solution)/shard_map/ppermute | solution.py:25
  24.5 3.0 %collective-permute-start.3 = (f32[16,1024]{1,0:T(8,128)S(1)}, f32[16,1024]{1,0:T(8,128)S(1)}, u32[]{:S(2)}, u32[]{:S(2)}) collective-permute-start(f32[16,1024]{1,0:T(8,128)S(1)} %multiply_reduce_fusion.1), channel_id=1, source_target_pairs={{0,24},{8,0},{16,8},{24,16},{32,56},{40,32},{48,40},{56,48},{64,88... | collective-permute-start | bytes 196616 | tf_op jit(solution)/shard_map/ppermute | solution.py:25
  28.5 1.1 reshape.75
  29.6 1.1 collective-permute-done.3
  30.7 3.8 %collective-permute-start.4 = (f32[16,1024]{1,0:T(8,128)S(1)}, f32[16,1024]{1,0:T(8,128)S(1)}, u32[]{:S(2)}, u32[]{:S(2)}) collective-permute-start(f32[16,1024]{1,0:T(8,128)S(1)} %multiply_add_fusion.2), channel_id=1, source_target_pairs={{0,32},{8,40},{16,48},{24,56},{32,64},{40,72},{48,80},{56,88},{64,... | collective-permute-start | bytes 196616 | tf_op jit(solution)/shard_map/ppermute | solution.py:25
  34.6 6.4 %collective-permute-start.5 = (f32[16,1024]{1,0:T(8,128)S(1)}, f32[16,1024]{1,0:T(8,128)S(1)}, u32[]{:S(2)}, u32[]{:S(2)}) collective-permute-start(f32[16,1024]{1,0:T(8,128)S(1)} %multiply_add_fusion.2), channel_id=1, source_target_pairs={{0,64},{8,72},{16,80},{24,88},{32,96},{40,104},{48,112},{56,120},{... | collective-permute-start | bytes 196616 | tf_op jit(solution)/shard_map/ppermute | solution.py:25
  41.0 1.9 %collective-permute-start.6 = (f32[16,1024]{1,0:T(8,128)S(1)}, f32[16,1024]{1,0:T(8,128)S(1)}, u32[]{:S(2)}, u32[]{:S(2)}) collective-permute-start(f32[16,1024]{1,0:T(8,128)S(1)} %multiply_add_fusion.2), channel_id=1, source_target_pairs={{0,96},{8,104},{16,112},{24,120},{32,0},{40,8},{48,16},{56,24},{64... | collective-permute-start | bytes 196616 | tf_op jit(solution)/shard_map/ppermute | solution.py:25
  43.1 1.3 collective-permute-done.5
  44.4 2.7 %collective-permute-done.6 = f32[16,1024]{1,0:T(8,128)S(1)} collective-permute-done((f32[16,1024]{1,0:T(8,128)S(1)}, f32[16,1024]{1,0:T(8,128)S(1)}, u32[]{:S(2)}, u32[]{:S(2)}) %collective-permute-start.6) | collective-permute-done | bytes 65568 | tf_op jit(solution)/shard_map/ppermute | solution.py:25
  47.2 9.1 %collective-permute-start.7 = (f32[16,1024]{1,0:T(8,128)S(1)}, f32[16,1024]{1,0:T(8,128)S(1)}, u32[]{:S(2)}, u32[]{:S(2)}) collective-permute-start(f32[16,1024]{1,0:T(8,128)S(1)} %multiply_add_fusion.1), channel_id=1, source_target_pairs={{0,128},{8,136},{16,144},{24,152},{32,160},{40,168},{48,176},{56,1... | collective-permute-start | bytes 196616 | tf_op jit(solution)/shard_map/ppermute | solution.py:25
  56.3 7.2 %collective-permute-start.8 = (f32[16,1024]{1,0:T(8,128)S(1)}, f32[16,1024]{1,0:T(8,128)S(1)}, u32[]{:S(2)}, u32[]{:S(2)}) collective-permute-start(f32[16,1024]{1,0:T(8,128)S(1)} %multiply_add_fusion.1), channel_id=1, source_target_pairs={{0,256},{8,264},{16,272},{24,280},{32,288},{40,296},{48,304},{56,3... | collective-permute-start | bytes 196616 | tf_op jit(solution)/shard_map/ppermute | solution.py:25
  63.4 5.5 %collective-permute-start.9 = (f32[16,1024]{1,0:T(8,128)S(1)}, f32[16,1024]{1,0:T(8,128)S(1)}, u32[]{:S(2)}, u32[]{:S(2)}) collective-permute-start(f32[16,1024]{1,0:T(8,128)S(1)} %multiply_add_fusion.1), channel_id=1, source_target_pairs={{0,384},{8,392},{16,400},{24,408},{32,416},{40,424},{48,432},{56,4... | collective-permute-start | bytes 196616 | tf_op jit(solution)/shard_map/ppermute | solution.py:25
  69.8 1.8 collective-permute-done.8
  71.5 4.0 %collective-permute-done.9 = f32[16,1024]{1,0:T(8,128)S(1)} collective-permute-done((f32[16,1024]{1,0:T(8,128)S(1)}, f32[16,1024]{1,0:T(8,128)S(1)}, u32[]{:S(2)}, u32[]{:S(2)}) %collective-permute-start.9) | collective-permute-done | bytes 65568 | tf_op jit(solution)/shard_map/ppermute | solution.py:25
  75.7 1.4 multiply_reduce_fusion
  77.2 1.2 broadcast_in_dim.11
  78.3 3.7 %all-to-all-start = ((bf16[8,64,1024]{2,1,0:T(8,128)(2,1)}), bf16[8,64,1024]{2,1,0:T(8,128)(2,1)S(1)}, u32[]{:S(2)}, u32[]{:S(2)}) async-start(bf16[8,64,1024]{2,1,0:T(8,128)(2,1)} %broadcast_in_dim.11), calls=%async_computation | async-start | bytes 2097152 | tf_op jit(solution)/shard_map/all_to_all | solution.py:108
  82.8 52.5 %all-gather.2.cloned.1.call-done = bf16[1024,512]{0,1:T(8,128)(2,1)} async-done(((bf16[1024,64]{0,1:T(8,128)(2,1)}), bf16[1024,512]{0,1:T(8,128)(2,1)}) %all-gather.2.cloned.1.call-update) | async-done | bytes 1048592 | tf_op jit(solution)/shard_map/all_gather | solution.py:50
  135.3 2.5 %convolution_bitcast_fusion = f32[8,8,64,64]{3,2,0,1:T(8,128)S(1)} fusion(bf16[1024,8,64,1]{0,2,1,3:T(8,128)(2,1)} %bitcast.45, bf16[8,64,1024]{2,1,0:T(8,128)(2,1)S(1)} %all-to-all-done), kind=kOutput, calls=%fused_computation.3 | convolution fusion | flops 536870912 | bytes 3145728 | tf_op jit(solution)/shard_map/ktc,cqo->qkto/dot_general | solution.py:109
  138.1 1.3 reshape.82
  139.4 19.1 %all_to_all.15 = f32[8,1,32768]{2,1,0:T(1,128)S(1)} all-to-all(f32[8,1,32768]{2,1,0:T(1,128)S(1)} %reshape.82), channel_id=1, replica_groups=mesh['chi'=8,'clo'=8,'tp'=8] {'tp'}, dimensions={0} | all-to-all | bytes 2097152 | tf_op jit(solution)/shard_map/all_to_all | solution.py:110
  159.1 3.1 %reduce = f32[8,32768]{1,0:T(8,128)S(1)} reduce(f32[8,1,32768]{2,1,0:T(1,128)S(1)} %all_to_all.15, f32[]{:T(128)} %broadcast.33), dimensions={1}, to_apply=%all_to_all.10.reduce_sub_computation | reduce | bytes 2097156 | tf_op jit(solution)/shard_map/all_to_all | solution.py:110
  162.2 0.8 reshape.83
  163.4 12.6 %all_to_all.16 = bf16[8,2,2048]{2,1,0:T(2,128)(2,1)S(1)} all-to-all(bf16[8,2,2048]{2,1,0:T(2,128)(2,1)S(1)} %reshape.84), channel_id=1, replica_groups=mesh['chi'=8,'clo'=8,'tp'=8] {'clo'}, dimensions={0} | all-to-all | bytes 131072 | tf_op jit(solution)/shard_map/all_to_all | solution.py:112
  176.3 0.8 reshape.78
  (38 shorter events, 5.2 us)
Async XLA Ops:
  7.4 6.2 %collective-permute-start = (bf16[3,2,1024]{2,1,0:T(2,128)(2,1)S(1)}, bf16[3,2,1024]{2,1,0:T(2,128)(2,1)S(1)}, u32[]{:S(2)}, u32[]{:S(2)}) collective-permute-start(bf16[3,2,1024]{2,1,0:T(2,128)(2,1)S(1)} %slice.29), channel_id=1, source_target_pairs={{0,8},{8,16},{16,24},{24,32},{32,40},{40,48},{48,56},{56,64},{64,7... | collective-permute-start | bytes 36872 | tf_op jit(solution)/shard_map/ppermute | solution.py:13
  13.6 13.9 %copy-start = (bf16[64,4096]{1,0:T(8,128)(2,1)S(1)}, bf16[64,4096]{1,0:T(8,128)(2,1)}, u32[]{:S(2)}) copy-start(bf16[64,4096]{1,0:T(8,128)(2,1)} %constant.139.clone) | copy-start | bytes 1572868
  16.2 13.4 %collective-permute-start.1 = (f32[16,1024]{1,0:T(8,128)S(1)}, f32[16,1024]{1,0:T(8,128)S(1)}, u32[]{:S(2)}, u32[]{:S(2)}) collective-permute-start(f32[16,1024]{1,0:T(8,128)S(1)} %multiply_reduce_fusion.1), channel_id=1, source_target_pairs={{0,8},{8,16},{16,24},{24,0},{32,40},{40,48},{48,56},{56,32},{64,72... | collective-permute-start | bytes 196616 | tf_op jit(solution)/shard_map/ppermute | solution.py:25
  19.7 9.9 %collective-permute-start.2 = (f32[16,1024]{1,0:T(8,128)S(1)}, f32[16,1024]{1,0:T(8,128)S(1)}, u32[]{:S(2)}, u32[]{:S(2)}) collective-permute-start(f32[16,1024]{1,0:T(8,128)S(1)} %multiply_reduce_fusion.1), channel_id=1, source_target_pairs={{0,16},{8,24},{16,0},{24,8},{32,48},{40,56},{48,32},{56,40},{64,80... | collective-permute-start | bytes 196616 | tf_op jit(solution)/shard_map/ppermute | solution.py:25
  24.5 6.2 %collective-permute-start.3 = (f32[16,1024]{1,0:T(8,128)S(1)}, f32[16,1024]{1,0:T(8,128)S(1)}, u32[]{:S(2)}, u32[]{:S(2)}) collective-permute-start(f32[16,1024]{1,0:T(8,128)S(1)} %multiply_reduce_fusion.1), channel_id=1, source_target_pairs={{0,24},{8,0},{16,8},{24,16},{32,56},{40,32},{48,40},{56,48},{64,88... | collective-permute-start | bytes 196616 | tf_op jit(solution)/shard_map/ppermute | solution.py:25
  30.7 12.3 %collective-permute-start.4 = (f32[16,1024]{1,0:T(8,128)S(1)}, f32[16,1024]{1,0:T(8,128)S(1)}, u32[]{:S(2)}, u32[]{:S(2)}) collective-permute-start(f32[16,1024]{1,0:T(8,128)S(1)} %multiply_add_fusion.2), channel_id=1, source_target_pairs={{0,32},{8,40},{16,48},{24,56},{32,64},{40,72},{48,80},{56,88},{64,... | collective-permute-start | bytes 196616 | tf_op jit(solution)/shard_map/ppermute | solution.py:25
  34.6 9.8 %collective-permute-start.5 = (f32[16,1024]{1,0:T(8,128)S(1)}, f32[16,1024]{1,0:T(8,128)S(1)}, u32[]{:S(2)}, u32[]{:S(2)}) collective-permute-start(f32[16,1024]{1,0:T(8,128)S(1)} %multiply_add_fusion.2), channel_id=1, source_target_pairs={{0,64},{8,72},{16,80},{24,88},{32,96},{40,104},{48,112},{56,120},{... | collective-permute-start | bytes 196616 | tf_op jit(solution)/shard_map/ppermute | solution.py:25
  41.0 6.2 %collective-permute-start.6 = (f32[16,1024]{1,0:T(8,128)S(1)}, f32[16,1024]{1,0:T(8,128)S(1)}, u32[]{:S(2)}, u32[]{:S(2)}) collective-permute-start(f32[16,1024]{1,0:T(8,128)S(1)} %multiply_add_fusion.2), channel_id=1, source_target_pairs={{0,96},{8,104},{16,112},{24,120},{32,0},{40,8},{48,16},{56,24},{64... | collective-permute-start | bytes 196616 | tf_op jit(solution)/shard_map/ppermute | solution.py:25
  47.2 22.6 %collective-permute-start.7 = (f32[16,1024]{1,0:T(8,128)S(1)}, f32[16,1024]{1,0:T(8,128)S(1)}, u32[]{:S(2)}, u32[]{:S(2)}) collective-permute-start(f32[16,1024]{1,0:T(8,128)S(1)} %multiply_add_fusion.1), channel_id=1, source_target_pairs={{0,128},{8,136},{16,144},{24,152},{32,160},{40,168},{48,176},{56,1... | collective-permute-start | bytes 196616 | tf_op jit(solution)/shard_map/ppermute | solution.py:25
  56.3 15.2 %collective-permute-start.8 = (f32[16,1024]{1,0:T(8,128)S(1)}, f32[16,1024]{1,0:T(8,128)S(1)}, u32[]{:S(2)}, u32[]{:S(2)}) collective-permute-start(f32[16,1024]{1,0:T(8,128)S(1)} %multiply_add_fusion.1), channel_id=1, source_target_pairs={{0,256},{8,264},{16,272},{24,280},{32,288},{40,296},{48,304},{56,3... | collective-permute-start | bytes 196616 | tf_op jit(solution)/shard_map/ppermute | solution.py:25
  63.4 12.1 %collective-permute-start.9 = (f32[16,1024]{1,0:T(8,128)S(1)}, f32[16,1024]{1,0:T(8,128)S(1)}, u32[]{:S(2)}, u32[]{:S(2)}) collective-permute-start(f32[16,1024]{1,0:T(8,128)S(1)} %multiply_add_fusion.1), channel_id=1, source_target_pairs={{0,384},{8,392},{16,400},{24,408},{32,416},{40,424},{48,432},{56,4... | collective-permute-start | bytes 196616 | tf_op jit(solution)/shard_map/ppermute | solution.py:25
  69.5 7.5 %copy-start.1 = (f32[1024]{0:T(1024)S(1)}, f32[1024]{0:T(1024)}, u32[]{:S(2)}) copy-start(f32[1024]{0:T(1024)} %param.11) | copy-start | bytes 12292
  78.3 57.0 %all-to-all-start = ((bf16[8,64,1024]{2,1,0:T(8,128)(2,1)}), bf16[8,64,1024]{2,1,0:T(8,128)(2,1)S(1)}, u32[]{:S(2)}, u32[]{:S(2)}) async-start(bf16[8,64,1024]{2,1,0:T(8,128)(2,1)} %broadcast_in_dim.11), calls=%async_computation | async-start | bytes 2097152 | tf_op jit(solution)/shard_map/all_to_all | solution.py:108
  82.1 53.2 %all-gather.2.cloned.1.call-start = ((), (), s32[]{:S(2)}) async-start(), calls=%async_computation.3 | async-start | bytes 1179648 | tf_op jit(solution)/shard_map/all_gather | solution.py:50
Sparse Core Ops, SparseCore 0:
  85.0 50.3 all-gather.1
where the time goes:
time: 185 us; the launch traced here: 184 us
  waiting for transfers between devices  64.1 us (35%)
  starting transfers between devices  52.4 us (28%)
  blocking collectives  31.7 us (17%)
  between operations  13.9 us (8%)
  local copies, waits for them, and re-layouts  9.62 us (5%)
  other arithmetic  8.77 us (5%)
  matrix products  3.41 us (2%)
    all_gather x1, waiting for transfers between devices, per_device(): weight = lax.all_gather(out_weight, 'chi', axis=1, tiled=True)  52.5 us
    ppermute x9, starting transfers between devices, digit_rotated(): return lax.ppermute(value, CTX, pairs)  45.1 us
    all_to_all x1, blocking collectives, per_device(): pieces = lax.all_to_all(partial, 'tp', 0, 0, tiled=True)  19.1 us
    all_to_all x1, blocking collectives, per_device(): back = lax.all_to_all(summed, 'clo', 0, 0, tiled=True)  12.6 us
    ppermute x9, waiting for transfers between devices, digit_rotated(): return lax.ppermute(value, CTX, pairs)  10.9 us
    all_to_all x1, starting transfers between devices, per_device(): tokens = lax.all_to_all(spread, 'clo', 0, 0, tiled=True)  3.75 us
  transfers between devices with their start and end apart: 12, of which 6 were waited for; matrix products, arithmetic and copies ran while one was open for 3% of the time, Pallas kernels for 0%

commit v1 on v0

--- a/solution.py
+++ b/solution.py
@@ -47,7 +47,9 @@
         clo = lax.axis_index("clo")
         me = chi * n_lo + clo
         tp = lax.axis_index("tp")
-        weight = lax.all_gather(out_weight, "chi", axis=1, tiled=True)
+        weight = jnp.concatenate(
+            lax.all_to_all(jnp.stack([out_weight] * lax.axis_size("chi")), "chi", 0, 0), axis=1
+        )
         weight = weight.reshape(chans, n_tp, -1)
         rim = shifted(features[:, rows - (taps - 1) :, :], CTX, n_ctx, 1)
         extended = jnp.concatenate([rim, features], axis=1)

time: 185 us -> 178 us (0.962)
  the two profiles are of different devices: /device:TPU:2 before, /device:TPU:64 now
where the time goes in v1:
time: 178 us; the launch traced here: 177 us
  starting transfers between devices  59.3 us (33%)
  waiting for transfers between devices  50.7 us (28%)
  blocking collectives  47.7 us (27%)
  local copies, waits for them, and re-layouts  8.98 us (5%)
  other arithmetic  6.51 us (4%)
  matrix products  3.4 us (2%)
    ppermute x1, waiting for transfers between devices, shifted(): return lax.ppermute(value, axis, pairs)  42.4 us
    ppermute x9, starting transfers between devices, digit_rotated(): return lax.ppermute(value, CTX, pairs)  41.1 us
    all_to_all x1, blocking collectives, per_device(): pieces = lax.all_to_all(partial, 'tp', 0, 0, tiled=True)  20.1 us
    all_to_all x1, blocking collectives, per_device(): tokens = lax.all_to_all(spread, 'clo', 0, 0, tiled=True)  18.7 us
    all_to_all x1, starting transfers between devices, per_device(): lax.all_to_all(jnp.stack([out_weight] * lax.axis_size('chi')), 'chi', 0, 0)  14.7 us
    all_to_all x1, blocking collectives, per_device(): back = lax.all_to_all(summed, 'clo', 0, 0, tiled=True)  8.89 us
    ppermute x9, waiting for transfers between devices, digit_rotated(): return lax.ppermute(value, CTX, pairs)  8.26 us
  transfers between devices with their start and end apart: 11, of which 6 were waited for; matrix products, arithmetic and copies ran while one was open for 4% of the time, Pallas kernels for 0%

profile of v1, /device:TPU:64, one launch (start us, length us, event | category | flops | bytes accessed | tf_op | source)
XLA Modules:
  0.0 177.2 jit_solution(11113809846797515461)
XLA Ops:
  0.0 2.1 %stack.2 = bf16[8,1024,64]{1,2,0:T(8,128)(2,1)} broadcast(bf16[1024,64]{0,1:T(8,128)(2,1)} %param.12), dimensions={1,2} | broadcast | bytes 1179648 | tf_op jit(solution)/shard_map/stack | solution.py:51
  2.1 14.7 %all-to-all-start.1 = ((bf16[8,1024,64]{1,2,0:T(8,128)(2,1)}), bf16[8,1024,64]{1,2,0:T(8,128)(2,1)}, u32[]{:S(2)}, u32[]{:S(2)}) async-start(bf16[8,1024,64]{1,2,0:T(8,128)(2,1)} %stack.2), calls=%async_computation.1 | async-start | bytes 2097152 | tf_op jit(solution)/shard_map/all_to_all | solution.py:51
  16.9 3.5 %collective-permute-start = (bf16[3,2,1024]{2,1,0:T(2,128)(2,1)S(1)}, bf16[3,2,1024]{2,1,0:T(2,128)(2,1)S(1)}, u32[]{:S(2)}, u32[]{:S(2)}) collective-permute-start(bf16[3,2,1024]{2,1,0:T(2,128)(2,1)S(1)} %slice.29), channel_id=1, source_target_pairs={{0,8},{8,16},{16,24},{24,32},{32,40},{40,48},{48,56},{56,64},{64,7... | collective-permute-start | bytes 36872 | tf_op jit(solution)/shard_map/ppermute | solution.py:13
  20.6 0.4 multiply_reduce_fusion.2
  21.5 42.4 %collective-permute-done = bf16[3,2,1024]{2,1,0:T(2,128)(2,1)S(1)} collective-permute-done((bf16[3,2,1024]{2,1,0:T(2,128)(2,1)S(1)}, bf16[3,2,1024]{2,1,0:T(2,128)(2,1)S(1)}, u32[]{:S(2)}, u32[]{:S(2)}) %collective-permute-start) | collective-permute-done | bytes 12320 | tf_op jit(solution)/shard_map/ppermute | solution.py:13
  64.3 0.7 multiply_reduce_fusion.1
  65.1 1.9 %collective-permute-start.1 = (f32[16,1024]{1,0:T(8,128)S(1)}, f32[16,1024]{1,0:T(8,128)S(1)}, u32[]{:S(2)}, u32[]{:S(2)}) collective-permute-start(f32[16,1024]{1,0:T(8,128)S(1)} %multiply_reduce_fusion.1), channel_id=1, source_target_pairs={{0,8},{8,16},{16,24},{24,0},{32,40},{40,48},{48,56},{56,32},{64,72... | collective-permute-start | bytes 196616 | tf_op jit(solution)/shard_map/ppermute | solution.py:25
  67.0 1.9 %collective-permute-start.2 = (f32[16,1024]{1,0:T(8,128)S(1)}, f32[16,1024]{1,0:T(8,128)S(1)}, u32[]{:S(2)}, u32[]{:S(2)}) collective-permute-start(f32[16,1024]{1,0:T(8,128)S(1)} %multiply_reduce_fusion.1), channel_id=1, source_target_pairs={{0,16},{8,24},{16,0},{24,8},{32,48},{40,56},{48,32},{56,40},{64,80... | collective-permute-start | bytes 196616 | tf_op jit(solution)/shard_map/ppermute | solution.py:25
  68.9 5.1 %collective-permute-start.3 = (f32[16,1024]{1,0:T(8,128)S(1)}, f32[16,1024]{1,0:T(8,128)S(1)}, u32[]{:S(2)}, u32[]{:S(2)}) collective-permute-start(f32[16,1024]{1,0:T(8,128)S(1)} %multiply_reduce_fusion.1), channel_id=1, source_target_pairs={{0,24},{8,0},{16,8},{24,16},{32,56},{40,32},{48,40},{56,48},{64,88... | collective-permute-start | bytes 196616 | tf_op jit(solution)/shard_map/ppermute | solution.py:25
  75.0 1.1 reshape.77
  76.2 0.9 collective-permute-done.3
  77.2 3.5 %collective-permute-start.4 = (f32[16,1024]{1,0:T(8,128)S(1)}, f32[16,1024]{1,0:T(8,128)S(1)}, u32[]{:S(2)}, u32[]{:S(2)}) collective-permute-start(f32[16,1024]{1,0:T(8,128)S(1)} %multiply_add_fusion.2), channel_id=1, source_target_pairs={{0,32},{8,40},{16,48},{24,56},{32,64},{40,72},{48,80},{56,88},{64,... | collective-permute-start | bytes 196616 | tf_op jit(solution)/shard_map/ppermute | solution.py:25
  80.7 1.9 %collective-permute-start.5 = (f32[16,1024]{1,0:T(8,128)S(1)}, f32[16,1024]{1,0:T(8,128)S(1)}, u32[]{:S(2)}, u32[]{:S(2)}) collective-permute-start(f32[16,1024]{1,0:T(8,128)S(1)} %multiply_add_fusion.2), channel_id=1, source_target_pairs={{0,64},{8,72},{16,80},{24,88},{32,96},{40,104},{48,112},{56,120},{... | collective-permute-start | bytes 196616 | tf_op jit(solution)/shard_map/ppermute | solution.py:25
  82.6 3.4 %collective-permute-start.6 = (f32[16,1024]{1,0:T(8,128)S(1)}, f32[16,1024]{1,0:T(8,128)S(1)}, u32[]{:S(2)}, u32[]{:S(2)}) collective-permute-start(f32[16,1024]{1,0:T(8,128)S(1)} %multiply_add_fusion.2), channel_id=1, source_target_pairs={{0,96},{8,104},{16,112},{24,120},{32,0},{40,8},{48,16},{56,24},{64... | collective-permute-start | bytes 196616 | tf_op jit(solution)/shard_map/ppermute | solution.py:25
  86.2 2.1 %collective-permute-done.5 = f32[16,1024]{1,0:T(8,128)S(1)} collective-permute-done((f32[16,1024]{1,0:T(8,128)S(1)}, f32[16,1024]{1,0:T(8,128)S(1)}, u32[]{:S(2)}, u32[]{:S(2)}) %collective-permute-start.5) | collective-permute-done | bytes 65568 | tf_op jit(solution)/shard_map/ppermute | solution.py:25
  88.3 0.5 collective-permute-done.6
  88.8 8.5 %collective-permute-start.7 = (f32[16,1024]{1,0:T(8,128)S(1)}, f32[16,1024]{1,0:T(8,128)S(1)}, u32[]{:S(2)}, u32[]{:S(2)}) collective-permute-start(f32[16,1024]{1,0:T(8,128)S(1)} %multiply_add_fusion.1), channel_id=1, source_target_pairs={{0,128},{8,136},{16,144},{24,152},{32,160},{40,168},{48,176},{56,1... | collective-permute-start | bytes 196616 | tf_op jit(solution)/shard_map/ppermute | solution.py:25
  97.3 9.3 %collective-permute-start.8 = (f32[16,1024]{1,0:T(8,128)S(1)}, f32[16,1024]{1,0:T(8,128)S(1)}, u32[]{:S(2)}, u32[]{:S(2)}) collective-permute-start(f32[16,1024]{1,0:T(8,128)S(1)} %multiply_add_fusion.1), channel_id=1, source_target_pairs={{0,256},{8,264},{16,272},{24,280},{32,288},{40,296},{48,304},{56,3... | collective-permute-start | bytes 196616 | tf_op jit(solution)/shard_map/ppermute | solution.py:25
  106.6 5.5 %collective-permute-start.9 = (f32[16,1024]{1,0:T(8,128)S(1)}, f32[16,1024]{1,0:T(8,128)S(1)}, u32[]{:S(2)}, u32[]{:S(2)}) collective-permute-start(f32[16,1024]{1,0:T(8,128)S(1)} %multiply_add_fusion.1), channel_id=1, source_target_pairs={{0,384},{8,392},{16,400},{24,408},{32,416},{40,424},{48,432},{56,4... | collective-permute-start | bytes 196616 | tf_op jit(solution)/shard_map/ppermute | solution.py:25
  112.1 0.6 fusion.11
  113.0 1.5 collective-permute-done.8
  114.5 3.2 %collective-permute-done.9 = f32[16,1024]{1,0:T(8,128)S(1)} collective-permute-done((f32[16,1024]{1,0:T(8,128)S(1)}, f32[16,1024]{1,0:T(8,128)S(1)}, u32[]{:S(2)}, u32[]{:S(2)}) %collective-permute-start.9) | collective-permute-done | bytes 65568 | tf_op jit(solution)/shard_map/ppermute | solution.py:25
  117.8 1.4 multiply_reduce_fusion
  119.5 18.7 %all_to_all.20 = bf16[8,64,1024]{2,1,0:T(8,128)(2,1)S(1)} all-to-all(bf16[8,64,1024]{2,1,0:T(8,128)(2,1)S(1)} %broadcast_in_dim.11), channel_id=1, replica_groups=mesh['chi'=8,'clo'=8,'tp'=8] {'clo'}, dimensions={0} | all-to-all | bytes 2097152 | tf_op jit(solution)/shard_map/all_to_all | solution.py:110
  138.2 2.5 %convolution_bitcast_fusion = f32[8,8,64,64]{3,2,0,1:T(8,128)S(1)} fusion(bf16[8,1024,64]{1,2,0:T(8,128)(2,1)} %all-to-all-done.1, bf16[8,64,1024]{2,1,0:T(8,128)(2,1)S(1)} %all_to_all.20), kind=kOutput, calls=%fused_computation.3 | convolution fusion | flops 536870912 | bytes 3145728 | tf_op jit(solution)/shard_map/ktc,cqo->qkto/dot_general | solution.py:111
  141.0 1.3 reshape.84
  142.3 20.1 %all_to_all.21 = f32[8,1,32768]{2,1,0:T(1,128)S(1)} all-to-all(f32[8,1,32768]{2,1,0:T(1,128)S(1)} %reshape.84), channel_id=1, replica_groups=mesh['chi'=8,'clo'=8,'tp'=8] {'tp'}, dimensions={0} | all-to-all | bytes 2097152 | tf_op jit(solution)/shard_map/all_to_all | solution.py:112
  162.4 0.5 broadcast.35
  162.9 3.1 %reduce = f32[8,32768]{1,0:T(8,128)S(1)} reduce(f32[8,1,32768]{2,1,0:T(1,128)S(1)} %all_to_all.21, f32[]{:T(128)} %broadcast.35), dimensions={1}, to_apply=%all_to_all.14.reduce_sub_computation | reduce | bytes 2097156 | tf_op jit(solution)/shard_map/all_to_all | solution.py:112
  166.0 0.8 reshape.85
  167.3 8.9 %all_to_all.22 = bf16[8,2,2048]{2,1,0:T(2,128)(2,1)S(1)} all-to-all(bf16[8,2,2048]{2,1,0:T(2,128)(2,1)S(1)} %reshape.86), channel_id=1, replica_groups=mesh['chi'=8,'clo'=8,'tp'=8] {'clo'}, dimensions={0} | all-to-all | bytes 131072 | tf_op jit(solution)/shard_map/all_to_all | solution.py:114
  176.4 0.8 reshape.80
  (45 shorter events, 3.4 us)
Async XLA Ops:
  0.0 16.9 %copy-start.1 = (bf16[3,64,1024]{2,1,0:T(8,128)(2,1)S(1)}, bf16[3,64,1024]{2,1,0:T(8,128)(2,1)}, u32[]{:S(2)}) copy-start(bf16[3,64,1024]{2,1,0:T(8,128)(2,1)} %param.7) | copy-start | bytes 1179652
  0.0 20.4 %copy-start.4 = (f32[64,16]{0,1:T(8,128)S(1)}, f32[64,16]{0,1:T(8,128)}, u32[]{:S(2)}) copy-start(f32[64,16]{0,1:T(8,128)} %param.10) | copy-start | bytes 12292
  0.0 20.4 %copy-start.3 = (f32[64,16]{0,1:T(8,128)S(1)}, f32[64,16]{0,1:T(8,128)}, u32[]{:S(2)}) copy-start(f32[64,16]{0,1:T(8,128)} %param.9) | copy-start | bytes 12292
  0.0 21.0 %copy-start.2 = (f32[3,3,1024]{2,1,0:T(4,128)S(1)}, f32[3,3,1024]{2,1,0:T(4,128)}, u32[]{:S(2)}) copy-start(f32[3,3,1024]{2,1,0:T(4,128)} %param.8) | copy-start | bytes 110596
  2.1 117.2 %all-to-all-start.1 = ((bf16[8,1024,64]{1,2,0:T(8,128)(2,1)}), bf16[8,1024,64]{1,2,0:T(8,128)(2,1)}, u32[]{:S(2)}, u32[]{:S(2)}) async-start(bf16[8,1024,64]{1,2,0:T(8,128)(2,1)} %stack.2), calls=%async_computation.1 | async-start | bytes 2097152 | tf_op jit(solution)/shard_map/all_to_all | solution.py:51
  16.9 47.1 %collective-permute-start = (bf16[3,2,1024]{2,1,0:T(2,128)(2,1)S(1)}, bf16[3,2,1024]{2,1,0:T(2,128)(2,1)S(1)}, u32[]{:S(2)}, u32[]{:S(2)}) collective-permute-start(bf16[3,2,1024]{2,1,0:T(2,128)(2,1)S(1)} %slice.29), channel_id=1, source_target_pairs={{0,8},{8,16},{16,24},{24,32},{32,40},{40,48},{48,56},{56,64},{64,7... | collective-permute-start | bytes 36872 | tf_op jit(solution)/shard_map/ppermute | solution.py:13
  21.5 52.5 %copy-start = (bf16[64,4096]{1,0:T(8,128)(2,1)S(1)}, bf16[64,4096]{1,0:T(8,128)(2,1)}, u32[]{:S(2)}) copy-start(bf16[64,4096]{1,0:T(8,128)(2,1)} %constant.139.clone) | copy-start | bytes 1572868
  65.1 11.1 %collective-permute-start.1 = (f32[16,1024]{1,0:T(8,128)S(1)}, f32[16,1024]{1,0:T(8,128)S(1)}, u32[]{:S(2)}, u32[]{:S(2)}) collective-permute-start(f32[16,1024]{1,0:T(8,128)S(1)} %multiply_reduce_fusion.1), channel_id=1, source_target_pairs={{0,8},{8,16},{16,24},{24,0},{32,40},{40,48},{48,56},{56,32},{64,72... | collective-permute-start | bytes 196616 | tf_op jit(solution)/shard_map/ppermute | solution.py:25
  67.0 9.2 %collective-permute-start.2 = (f32[16,1024]{1,0:T(8,128)S(1)}, f32[16,1024]{1,0:T(8,128)S(1)}, u32[]{:S(2)}, u32[]{:S(2)}) collective-permute-start(f32[16,1024]{1,0:T(8,128)S(1)} %multiply_reduce_fusion.1), channel_id=1, source_target_pairs={{0,16},{8,24},{16,0},{24,8},{32,48},{40,56},{48,32},{56,40},{64,80... | collective-permute-start | bytes 196616 | tf_op jit(solution)/shard_map/ppermute | solution.py:25
  68.9 8.2 %collective-permute-start.3 = (f32[16,1024]{1,0:T(8,128)S(1)}, f32[16,1024]{1,0:T(8,128)S(1)}, u32[]{:S(2)}, u32[]{:S(2)}) collective-permute-start(f32[16,1024]{1,0:T(8,128)S(1)} %multiply_reduce_fusion.1), channel_id=1, source_target_pairs={{0,24},{8,0},{16,8},{24,16},{32,56},{40,32},{48,40},{56,48},{64,88... | collective-permute-start | bytes 196616 | tf_op jit(solution)/shard_map/ppermute | solution.py:25
  77.2 9.0 %collective-permute-start.4 = (f32[16,1024]{1,0:T(8,128)S(1)}, f32[16,1024]{1,0:T(8,128)S(1)}, u32[]{:S(2)}, u32[]{:S(2)}) collective-permute-start(f32[16,1024]{1,0:T(8,128)S(1)} %multiply_add_fusion.2), channel_id=1, source_target_pairs={{0,32},{8,40},{16,48},{24,56},{32,64},{40,72},{48,80},{56,88},{64,... | collective-permute-start | bytes 196616 | tf_op jit(solution)/shard_map/ppermute | solution.py:25
  80.7 7.6 %collective-permute-start.5 = (f32[16,1024]{1,0:T(8,128)S(1)}, f32[16,1024]{1,0:T(8,128)S(1)}, u32[]{:S(2)}, u32[]{:S(2)}) collective-permute-start(f32[16,1024]{1,0:T(8,128)S(1)} %multiply_add_fusion.2), channel_id=1, source_target_pairs={{0,64},{8,72},{16,80},{24,88},{32,96},{40,104},{48,112},{56,120},{... | collective-permute-start | bytes 196616 | tf_op jit(solution)/shard_map/ppermute | solution.py:25
  82.6 6.2 %collective-permute-start.6 = (f32[16,1024]{1,0:T(8,128)S(1)}, f32[16,1024]{1,0:T(8,128)S(1)}, u32[]{:S(2)}, u32[]{:S(2)}) collective-permute-start(f32[16,1024]{1,0:T(8,128)S(1)} %multiply_add_fusion.2), channel_id=1, source_target_pairs={{0,96},{8,104},{16,112},{24,120},{32,0},{40,8},{48,16},{56,24},{64... | collective-permute-start | bytes 196616 | tf_op jit(solution)/shard_map/ppermute | solution.py:25
  88.8 24.2 %collective-permute-start.7 = (f32[16,1024]{1,0:T(8,128)S(1)}, f32[16,1024]{1,0:T(8,128)S(1)}, u32[]{:S(2)}, u32[]{:S(2)}) collective-permute-start(f32[16,1024]{1,0:T(8,128)S(1)} %multiply_add_fusion.1), channel_id=1, source_target_pairs={{0,128},{8,136},{16,144},{24,152},{32,160},{40,168},{48,176},{56,1... | collective-permute-start | bytes 196616 | tf_op jit(solution)/shard_map/ppermute | solution.py:25
  97.3 17.2 %collective-permute-start.8 = (f32[16,1024]{1,0:T(8,128)S(1)}, f32[16,1024]{1,0:T(8,128)S(1)}, u32[]{:S(2)}, u32[]{:S(2)}) collective-permute-start(f32[16,1024]{1,0:T(8,128)S(1)} %multiply_add_fusion.1), channel_id=1, source_target_pairs={{0,256},{8,264},{16,272},{24,280},{32,288},{40,296},{48,304},{56,3... | collective-permute-start | bytes 196616 | tf_op jit(solution)/shard_map/ppermute | solution.py:25
  106.6 11.1 %collective-permute-start.9 = (f32[16,1024]{1,0:T(8,128)S(1)}, f32[16,1024]{1,0:T(8,128)S(1)}, u32[]{:S(2)}, u32[]{:S(2)}) collective-permute-start(f32[16,1024]{1,0:T(8,128)S(1)} %multiply_add_fusion.1), channel_id=1, source_target_pairs={{0,384},{8,392},{16,400},{24,408},{32,416},{40,424},{48,432},{56,4... | collective-permute-start | bytes 196616 | tf_op jit(solution)/shard_map/ppermute | solution.py:25
  112.8 6.5 %copy-start.5 = (f32[1024]{0:T(1024)S(1)}, f32[1024]{0:T(1024)}, u32[]{:S(2)}) copy-start(f32[1024]{0:T(1024)} %param.11) | copy-start | bytes 12292
